TPU v7x, 128 devices: a whole 4x4x4 slice. The times are simulated.
128 devices in a mesh: frow: 16 (over y, z), fcol: 8 (over x, core).
Axes of the slice: x: 4, y: 4, z: 4, core: 2. Of those that a mesh axis runs over, the one named last changes fastest.
Arguments:
- front_orig: float32 [16, 1024, 8, 2048], P('frow', None, 'fcol'), may hold values from -0.1 to 45, as said below
- child_tiles: bfloat16 [8192, 128, 128], P(('frow', 'fcol')), may hold values from -0.25 to 0.25
- tile_target: int32 [8192, 2], P(('frow', 'fcol')), may hold values from 0 to 127, as said below
- tile_rows: int32 [8192, 128], P(('frow', 'fcol')), may hold values from 0 to 127, each once within a row
- tile_cols: int32 [8192, 128], P(('frow', 'fcol')), may hold values from 0 to 127, each once within a row
Outputs:
- front_out: float32 [16, 1024, 8, 2048], P('frow', None, 'fcol')
Inputs may be any that keep to these rules, and one draw needn't show every extreme that they name: `front_orig`: Symmetric; the lower triangle of the front after every tile is added defines a positive definite matrix. `tile_target`: rows come 64 to a device in device order. Column 0 is the owner, frow index times 8 plus fcol index; column 1 the local block on that owner, local block row times 16 plus local block column; the block lies on or below the front's block diagonal. At most 2 tiles of one device go to one owner, and one owner receives exactly 2 from every device.
All inputs are finite; a program needn't handle non-finite values.
Results may differ from a plain program's by a relative error of at most 0.0003.
Values may be sent and summed in bfloat16 or wider, within the bound.
No kernel may reach another device: no remote copies, remote signals or barrier semaphores. Data moves between devices by JAX's collectives and lax.ppermute only.
A program may use at most 128 MiB of HBM per device.

v0:
```python
import jax
import jax.numpy as jnp
from jax import lax
from jax.sharding import PartitionSpec as P

PW = 512
NPANEL = 2
CAP = 2


def as_sent(x):
    return jax.tree.map(lambda a: a.astype(jnp.bfloat16) if a.dtype == jnp.float32 else a, x)


def broadcast(block, axis, source):
    block = jnp.where(lax.axis_index(axis) == source, block, jnp.zeros_like(block))
    return lax.psum(block, axis)


def place_tiles(received):
    tile_block, perm_block, target_block = received
    width = tile_block.shape[-1]
    positions = jnp.arange(width, dtype=jnp.int32)
    row_onehot = (perm_block[:, :, 0, None, :] == positions[:, None]).astype(jnp.bfloat16)
    col_onehot = (perm_block[:, :, 1, None, :] == positions[:, None]).astype(jnp.bfloat16)
    moved = jnp.einsum(
        "abxi,abij->abxj", row_onehot, tile_block, preferred_element_type=jnp.float32
    ).astype(jnp.bfloat16)
    placed = jnp.einsum(
        "abxj,abyj->abxy", moved, col_onehot, preferred_element_type=jnp.float32
    ).astype(jnp.bfloat16)
    return (placed, target_block)


def subtract_product(matrix, row_factor, col_factor):
    product = jnp.dot(
        row_factor,
        col_factor.T,
        precision=lax.Precision.HIGHEST,
        preferred_element_type=jnp.float32,
    )
    return matrix - product


def shards(front_orig, child_tiles, tile_target, tile_rows, tile_cols):
    row_devs = lax.axis_size("frow")
    col_devs = lax.axis_size("fcol")
    owners = row_devs * col_devs
    row_here = lax.axis_index("frow")
    col_here = lax.axis_index("fcol")
    width = child_tiles.shape[1]
    held = child_tiles.shape[0]
    slot_count = owners * CAP
    owner_of = tile_target[:, 0]
    block_of = tile_target[:, 1]
    tile_order = jnp.arange(held, dtype=jnp.int32)
    same_owner = owner_of[:, None] == owner_of[None, :]
    earlier = tile_order[None, :] < tile_order[:, None]
    rank_of = jnp.sum(jnp.where(same_owner & earlier, 1, 0), axis=1).astype(jnp.int32)
    slot_of = owner_of * CAP + rank_of
    slot_match = slot_of[None, :] == jnp.arange(slot_count, dtype=jnp.int32)[:, None]
    source_tile = jnp.sum(jnp.where(slot_match, tile_order[None, :], 0), axis=1)
    filled = jnp.any(slot_match, axis=1)
    send_tiles = jnp.where(
        filled[:, None, None],
        jnp.take(child_tiles, source_tile, axis=0),
        jnp.zeros((), jnp.bfloat16),
    )
    send_perms = jnp.stack(
        [jnp.take(tile_rows, source_tile, axis=0), jnp.take(tile_cols, source_tile, axis=0)], axis=1
    )
    send_blocks = jnp.take(block_of, source_tile, axis=0)
    placed, blocks_in = place_tiles(
        (
            lax.all_to_all(
                send_tiles.reshape(owners, CAP, width, width),
                ("frow", "fcol"),
                split_axis=0,
                concat_axis=0,
                tiled=True,
            ),
            lax.all_to_all(
                send_perms.reshape(owners, CAP, 2, width),
                ("frow", "fcol"),
                split_axis=0,
                concat_axis=0,
                tiled=True,
            ),
            lax.all_to_all(
                send_blocks.reshape(owners, CAP),
                ("frow", "fcol"),
                split_axis=0,
                concat_axis=0,
                tiled=True,
            ),
        )
    )
    local = front_orig[0, :, 0, :]
    row_blocks = local.shape[0] // width
    col_blocks = local.shape[1] // width
    block_ids = jnp.arange(row_blocks * col_blocks, dtype=jnp.int32)
    block_onehot = (blocks_in.reshape(1, slot_count) == block_ids[:, None]).astype(jnp.bfloat16)
    summed = jnp.dot(
        block_onehot, placed.reshape(slot_count, width * width), preferred_element_type=jnp.float32
    )
    added = (
        summed.reshape(row_blocks, col_blocks, width, width)
        .transpose(0, 2, 1, 3)
        .reshape(local.shape)
    )
    matrix = local + added
    local_rows = jnp.arange(local.shape[0], dtype=jnp.int32)
    local_cols = jnp.arange(local.shape[1], dtype=jnp.int32)
    global_rows = (local_rows // width * row_devs + row_here) * width + local_rows % width
    global_cols = (local_cols // width * col_devs + col_here) * width + local_cols % width
    panel_blocks = PW // width
    ratio = row_devs // col_devs
    for panel_idx in range(NPANEL):
        start = panel_idx * PW
        stop = start + PW
        first_block = panel_idx * panel_blocks
        col_slot = first_block // col_devs
        col_first = first_block % col_devs
        row_slot = first_block // row_devs
        row_first = first_block % row_devs
        own_column = matrix[:, col_slot * width : (col_slot + 1) * width]
        wide_panel = lax.all_gather(
            own_column.astype(jnp.bfloat16), "fcol", axis=1, tiled=True
        ).astype(own_column.dtype)
        panel = wide_panel[:, col_first * width : col_first * width + PW]
        diag_rows = lax.all_gather(
            panel[row_slot * width : (row_slot + 1) * width].astype(jnp.bfloat16),
            "frow",
            axis=0,
            tiled=True,
        ).astype(jnp.float32)
        diag_block = diag_rows[row_first * width : row_first * width + PW]
        symmetric = jnp.tril(diag_block) + jnp.tril(diag_block, -1).T
        factor = jnp.linalg.cholesky(symmetric)
        solved = lax.linalg.triangular_solve(
            factor, panel, left_side=False, lower=True, transpose_a=True
        )
        below = (global_rows >= stop)[:, None]
        inside = (global_rows >= start)[:, None]
        factor_rows = jnp.take(factor, jnp.clip(global_rows - start, 0, PW - 1), axis=0)
        new_panel = jnp.where(below, solved, jnp.where(inside, factor_rows, 0.0))
        row_factor = jnp.where(below, solved, 0.0)
        stacked = row_factor.reshape(row_blocks, width, PW)
        pieces = []
        for offset in range(ratio):
            pieces.append(
                broadcast(as_sent(stacked), "frow", col_here + col_devs * offset).astype(
                    stacked.dtype
                )
            )
        col_factor = jnp.stack(pieces, axis=1).reshape(local.shape[1], PW)
        matrix = subtract_product(matrix, row_factor, col_factor)
        in_panel = (col_here >= col_first) & (col_here < col_first + panel_blocks)
        shift_cols = jnp.clip(col_here - col_first, 0, panel_blocks - 1) * width
        own_part = lax.dynamic_slice_in_dim(new_panel, shift_cols, width, axis=1)
        current = matrix[:, col_slot * width : (col_slot + 1) * width]
        matrix = matrix.at[:, col_slot * width : (col_slot + 1) * width].set(
            jnp.where(in_panel, own_part, current)
        )
    lower_part = global_rows[:, None] >= global_cols[None, :]
    result = jnp.where(lower_part, matrix, 0.0)
    return result[None, :, None, :]


def solution(mesh):
    return jax.shard_map(
        shards,
        mesh=mesh,
        in_specs=(
            P("frow", None, "fcol", None),
            P(("frow", "fcol"), None, None),
            P(("frow", "fcol"), None),
            P(("frow", "fcol"), None),
            P(("frow", "fcol"), None),
        ),
        out_specs=P("frow", None, "fcol", None),
        check_vma=False,
    )
```

profile of v0, /device:TPU:0, one launch (start us, length us, event | category | flops | bytes accessed | tf_op | source)
XLA Modules:
  0.0 935.2 jit_solution(13525251485987118323)
XLA Ops:
  11.2 11.1 %all-to-all-start = ((s32[128,1,2]{2,1,0:T(1,128)}), s32[128,1,2]{2,1,0:T(1,128)S(1)}, u32[]{:S(2)}, u32[]{:S(2)}) async-start(s32[128,1,2]{2,1,0:T(1,128)} %bitcast.4), calls=%async_computation | async-start | bytes 131072 | tf_op jit(solution)/shard_map/all_to_all | solution.py:89
  33.7 9.8 %all-to-all-start.1 = ((s32[128,2,2,128]{3,1,2,0:T(2,128)}), s32[128,2,2,128]{3,1,2,0:T(2,128)S(1)}, u32[]{:S(2)}, u32[]{:S(2)}) async-start(s32[128,2,2,128]{3,1,2,0:T(2,128)} %pad_add_fusion), calls=%async_computation.1 | async-start | bytes 524288 | tf_op jit(solution)/shard_map/all_to_all | solution.py:82
  62.8 99.1 %all-to-all-done.2 = bf16[128,2,128,128]{3,2,1,0:T(8,128)(2,1)} async-done(((bf16[128,2,128,128]{3,2,1,0:T(8,128)(2,1)}), bf16[128,2,128,128]{3,2,1,0:T(8,128)(2,1)}, u32[]{:S(2)}, u32[]{:S(2)}) %all-to-all-start.2) | async-done | bytes 8388640 | tf_op jit(solution)/shard_map/all_to_all | solution.py:75
  161.9 13.3 %fusion.6 = bf16[128,2,128,128]{3,2,1,0:T(8,128)(2,1)} fusion(s32[128,2,128]{2,1,0:T(2,128)S(1)} %get-tuple-element.84, bf16[128,2,128,128]{3,2,1,0:T(8,128)(2,1)} %all-to-all-done.2, s32[128,2,128]{2,1,0:T(2,128)S(1)} %get-tuple-element.83), kind=kOutput, calls=%fused_computation.21 | convolution fusion | flops 2164260864 | bytes 17039360 | tf_op jit(solution)/shard_map/abxj,abyj->abxy/dot_general | solution.py:29
  175.2 34.5 %copy.135 = bf16[32,8,128,128]{3,1,2,0:T(8,128)(2,1)} copy(bf16[32,8,128,128]{3,2,1,0:T(8,128)(2,1)} %bitcast.182) | data formatting | bytes 16777216
  209.6 11.9 %copy.86 = bf16[16384,256]{1,0:T(8,128)(2,1)} copy(bf16[16384,256]{0,1:T(8,128)(2,1)} %bitcast.168) | data formatting | bytes 16777216 | tf_op jit(solution)/shard_map/dot_general | solution.py:103
  231.0 17.6 %bitcast_add_fusion = f32[1024,2048]{1,0:T(8,128)} fusion(f32[128,8,16,128]{3,2,1,0:T(8,128)} %bitcast.179, f32[1,1024,1,2048]{3,2,1,0:T(1,128)} %param.16), kind=kLoop, calls=%fused_computation.14 | loop fusion | flops 2097152 | bytes 25165824 | tf_op jit(solution)/shard_map/add | solution.py:111
  250.4 31.1 %all-gather.5.cloned.1.call-done = bf16[1024,1024]{1,0:T(8,128)(2,1)} async-done(((bf16[1024,128]{1,0:T(8,128)(2,1)}), bf16[1024,1024]{1,0:T(8,128)(2,1)}) %all-gather.5.cloned.1.call-update) | async-done | bytes 2097168 | tf_op jit(solution)/shard_map/all_gather | solution.py:127
  286.4 43.5 %all-gather.7.cloned.1.call-done = bf16[2048,512]{1,0:T(8,128)(2,1)} async-done(((bf16[128,512]{1,0:T(8,128)(2,1)}), bf16[2048,512]{1,0:T(8,128)(2,1)}) %all-gather.7.cloned.1.call-update) | async-done | bytes 2097168 | tf_op jit(solution)/shard_map/all_gather | solution.py:131
  333.3 11.7 %cholesky.286 = f32[128,128]{1,0:T(8,128)S(1)} custom-call(f32[128,128]{1,0:T(8,128)S(1)} %cholesky.426), custom_call_target="Cholesky" | custom-call | tf_op jit(solution)/shard_map/jit(cholesky)/cholesky | solution.py:139
  345.2 9.8 %custom-call.27 = f32[1,128,128]{1,2,0:T(8,128)S(1)} custom-call(f32[1,128,128]{2,1,0:T(8,128)S(1)} %get-tuple-element.104), custom_call_target="InvertDiagBlocksLowerTriangular" | custom-call | tf_op jit(solution)/shard_map/jit(cholesky)/cholesky | solution.py:139
  355.7 11.7 %cholesky.305 = f32[128,128]{1,0:T(8,128)S(1)} custom-call(f32[128,128]{1,0:T(8,128)S(1)} %cholesky.430), custom_call_target="Cholesky" | custom-call | tf_op jit(solution)/shard_map/jit(cholesky)/cholesky | solution.py:139
  367.4 10.0 %custom-call.28 = f32[1,128,128]{1,2,0:T(8,128)S(1)} custom-call(f32[1,128,128]{2,1,0:T(8,128)S(1)} %get-tuple-element.101), custom_call_target="InvertDiagBlocksLowerTriangular" | custom-call | tf_op jit(solution)/shard_map/jit(cholesky)/cholesky | solution.py:139
  378.1 11.7 %cholesky.326 = f32[128,128]{1,0:T(8,128)S(1)} custom-call(f32[128,128]{1,0:T(8,128)S(1)} %cholesky.435), custom_call_target="Cholesky" | custom-call | tf_op jit(solution)/shard_map/jit(cholesky)/cholesky | solution.py:139
  389.8 9.8 %custom-call.29 = f32[1,128,128]{1,2,0:T(8,128)S(1)} custom-call(f32[1,128,128]{2,1,0:T(8,128)S(1)} %get-tuple-element.98), custom_call_target="InvertDiagBlocksLowerTriangular" | custom-call | tf_op jit(solution)/shard_map/jit(cholesky)/cholesky | solution.py:139
  400.2 12.1 %cholesky.343 = f32[128,128]{1,0:T(8,128)S(1)} custom-call(f32[128,128]{1,0:T(8,128)S(1)} %convolution_subtract_fusion.11), custom_call_target="Cholesky" | custom-call | tf_op jit(solution)/shard_map/jit(cholesky)/cholesky | solution.py:139
  424.8 39.3 %custom-call.30 = f32[4,128,128]{1,2,0:T(8,128)S(1)} custom-call(f32[4,128,128]{2,1,0:T(8,128)S(1)} %get-tuple-element.47), custom_call_target="InvertDiagBlocksLowerTriangular" | custom-call | tf_op jit(solution)/shard_map/triangular_solve/custom-call.3 | solution.py:140
  485.1 82.8 %all-reduce.8.cloned.1.call-done = (bf16[8,1,128,512]{3,2,1,0:T(8,128)(2,1)}, bf16[8,1,128,512]{3,2,1,0:T(8,128)(2,1)}) async-done(((bf16[8,1,128,512]{3,2,1,0:T(8,128)(2,1)}, bf16[8,1,128,512]{3,2,1,0:T(8,128)(2,1)}), (bf16[8,1,128,512]{3,2,1,0:T(8,128)(2,1)}, bf16[8,1,128,512]{3,2,1,0:T(8,128)(2,1)})) %all-reduce.8.cloned.1.call-update) | async-done | bytes 2097168 | tf_op jit(solution)/shard_map/psum | solution.py:17
  569.7 9.9 %convolution_subtract_fusion.1 = f32[1024,2048]{1,0:T(8,128)S(1)} fusion(f32[1024,2048]{1,0:T(8,128)} %bitcast_add_fusion, bf16[2048,512]{1,0:T(8,128)(2,1)S(1)} %bitcast.180, pred[1024]{0:T(1024)(128)(4,1)S(1)} %get-tuple-element.118, f32[1024,128]{1,0:T(8,128)S(1)} %fusion.78, f32[1024,128]{1,0:T(8,128)S(1)} %fusion.79, f32[1024,128]{1,0:T(8,128)S(1)} %fusion.80, ...), kind=kOutput, calls=%fused_computation.23 | convolution fusion | flops 12889096192 | bytes 20972544 | tf_op jit(solution)/shard_map/dot_general | solution.py:36
  586.4 26.8 %all-gather.9.cloned.1.call-done = bf16[1024,1024]{1,0:T(8,128)(2,1)} async-done(((bf16[1024,128]{1,0:T(8,128)(2,1)}), bf16[1024,1024]{1,0:T(8,128)(2,1)}) %all-gather.9.cloned.1.call-update) | async-done | bytes 2097168 | tf_op jit(solution)/shard_map/all_gather | solution.py:127
  618.3 43.4 %all-gather.11.cloned.1.call-done = bf16[2048,512]{1,0:T(8,128)(2,1)} async-done(((bf16[128,512]{1,0:T(8,128)(2,1)}), bf16[2048,512]{1,0:T(8,128)(2,1)}) %all-gather.11.cloned.1.call-update) | async-done | bytes 2097168 | tf_op jit(solution)/shard_map/all_gather | solution.py:131
  665.1 11.7 %cholesky.358 = f32[128,128]{1,0:T(8,128)S(1)} custom-call(f32[128,128]{1,0:T(8,128)S(1)} %cholesky.439), custom_call_target="Cholesky" | custom-call | tf_op jit(solution)/shard_map/jit(cholesky)/cholesky | solution.py:139
  677.0 9.8 %custom-call.31 = f32[1,128,128]{1,2,0:T(8,128)S(1)} custom-call(f32[1,128,128]{2,1,0:T(8,128)S(1)} %get-tuple-element.94), custom_call_target="InvertDiagBlocksLowerTriangular" | custom-call | tf_op jit(solution)/shard_map/jit(cholesky)/cholesky | solution.py:139
  687.5 11.9 %cholesky.377 = f32[128,128]{1,0:T(8,128)S(1)} custom-call(f32[128,128]{1,0:T(8,128)S(1)} %cholesky.443), custom_call_target="Cholesky" | custom-call | tf_op jit(solution)/shard_map/jit(cholesky)/cholesky | solution.py:139
  699.4 9.8 %custom-call.32 = f32[1,128,128]{1,2,0:T(8,128)S(1)} custom-call(f32[1,128,128]{2,1,0:T(8,128)S(1)} %get-tuple-element.91), custom_call_target="InvertDiagBlocksLowerTriangular" | custom-call | tf_op jit(solution)/shard_map/jit(cholesky)/cholesky | solution.py:139
  709.9 11.7 %cholesky.398 = f32[128,128]{1,0:T(8,128)S(1)} custom-call(f32[128,128]{1,0:T(8,128)S(1)} %cholesky.448), custom_call_target="Cholesky" | custom-call | tf_op jit(solution)/shard_map/jit(cholesky)/cholesky | solution.py:139
  721.6 9.8 %custom-call.33 = f32[1,128,128]{1,2,0:T(8,128)S(1)} custom-call(f32[1,128,128]{2,1,0:T(8,128)S(1)} %get-tuple-element.88), custom_call_target="InvertDiagBlocksLowerTriangular" | custom-call | tf_op jit(solution)/shard_map/jit(cholesky)/cholesky | solution.py:139
  732.0 12.1 %cholesky.415 = f32[128,128]{1,0:T(8,128)S(1)} custom-call(f32[128,128]{1,0:T(8,128)S(1)} %convolution_subtract_fusion.10), custom_call_target="Cholesky" | custom-call | tf_op jit(solution)/shard_map/jit(cholesky)/cholesky | solution.py:139
  757.6 39.3 %custom-call.34 = f32[4,128,128]{1,2,0:T(8,128)S(1)} custom-call(f32[4,128,128]{2,1,0:T(8,128)S(1)} %get-tuple-element.48), custom_call_target="InvertDiagBlocksLowerTriangular" | custom-call | tf_op jit(solution)/shard_map/triangular_solve/custom-call.3 | solution.py:140
  819.1 81.6 %all-reduce.6.cloned.1.call-done = (bf16[8,1,128,512]{3,2,1,0:T(8,128)(2,1)}, bf16[8,1,128,512]{3,2,1,0:T(8,128)(2,1)}) async-done(((bf16[8,1,128,512]{3,2,1,0:T(8,128)(2,1)}, bf16[8,1,128,512]{3,2,1,0:T(8,128)(2,1)}), (bf16[8,1,128,512]{3,2,1,0:T(8,128)(2,1)}, bf16[8,1,128,512]{3,2,1,0:T(8,128)(2,1)})) %all-reduce.6.cloned.1.call-update) | async-done | bytes 2097168 | tf_op jit(solution)/shard_map/psum | solution.py:17
  902.4 10.0 %convolution_subtract_fusion = f32[1024,2048]{1,0:T(8,128)S(1)} fusion(f32[1024,2048]{1,0:T(8,128)} %constant_dynamic-update-slice_fusion.2, bf16[2048,512]{1,0:T(8,128)(2,1)S(1)} %bitcast.181, pred[1024]{0:T(1024)(128)(4,1)S(1)} %get-tuple-element.117, f32[1024,128]{1,0:T(8,128)S(1)} %fusion.72, f32[1024,128]{1,0:T(8,128)S(1)} %fusion.73, ...), kind=kOutput, calls=%fused_computation.22 | convolution fusion | flops 12889096192 | bytes 20972544 | tf_op jit(solution)/shard_map/dot_general | solution.py:36
  915.6 12.5 %copy.111 = f32[1,1024,1,2048]{3,2,1,0:T(1,128)} copy(f32[1,1024,1,2048]{3,1,2,0:T(8,128)S(1)} %select_bitcast_fusion) | data formatting | bytes 16777216 | tf_op jit(solution)/shard_map/broadcast_in_dim | solution.py:167
  (178 shorter events, 160.4 us)
Async XLA Ops:
  6.5 18.5 %copy-start = (bf16[64,128,128]{2,1,0:T(8,128)(2,1)S(1)}, bf16[64,128,128]{2,1,0:T(8,128)(2,1)}, u32[]{:S(2)}) copy-start(bf16[64,128,128]{2,1,0:T(8,128)(2,1)} %param.17) | copy-start | bytes 6291460
  6.5 16.0 %copy-start.3 = (s32[64,128]{1,0:T(8,128)S(1)}, s32[64,128]{1,0:T(8,128)}, u32[]{:S(2)}) copy-start(s32[64,128]{1,0:T(8,128)} %param.19) | copy-start | bytes 98308
  6.5 16.7 %copy-start.4 = (s32[64,128]{1,0:T(8,128)S(1)}, s32[64,128]{1,0:T(8,128)}, u32[]{:S(2)}) copy-start(s32[64,128]{1,0:T(8,128)} %param.20) | copy-start | bytes 98308
  11.2 22.5 %all-to-all-start = ((s32[128,1,2]{2,1,0:T(1,128)}), s32[128,1,2]{2,1,0:T(1,128)S(1)}, u32[]{:S(2)}, u32[]{:S(2)}) async-start(s32[128,1,2]{2,1,0:T(1,128)} %bitcast.4), calls=%async_computation | async-start | bytes 131072 | tf_op jit(solution)/shard_map/all_to_all | solution.py:89
  33.7 20.5 %all-to-all-start.1 = ((s32[128,2,2,128]{3,1,2,0:T(2,128)}), s32[128,2,2,128]{3,1,2,0:T(2,128)S(1)}, u32[]{:S(2)}, u32[]{:S(2)}) async-start(s32[128,2,2,128]{3,1,2,0:T(2,128)} %pad_add_fusion), calls=%async_computation.1 | async-start | bytes 524288 | tf_op jit(solution)/shard_map/all_to_all | solution.py:82
  54.2 107.7 %all-to-all-start.2 = ((bf16[128,2,128,128]{3,2,1,0:T(8,128)(2,1)}), bf16[128,2,128,128]{3,2,1,0:T(8,128)(2,1)}, u32[]{:S(2)}, u32[]{:S(2)}) async-start(bf16[128,2,128,128]{3,2,1,0:T(8,128)(2,1)} %select_select_fusion), calls=%async_computation.2 | async-start | bytes 16777216 | tf_op jit(solution)/shard_map/all_to_all | solution.py:75
  61.3 220.2 %all-gather.5.cloned.1.call-start = ((), (), s32[]{:S(2)}) async-start(), calls=%async_computation.3 | async-start | bytes 2359296 | tf_op jit(solution)/shard_map/all_gather | solution.py:127
  250.3 79.6 %all-gather.7.cloned.1.call-start = ((), (), s32[]{:S(2)}) async-start(), calls=%async_computation.4 | async-start | bytes 2228224 | tf_op jit(solution)/shard_map/all_gather | solution.py:131
  283.0 284.9 %all-reduce.8.cloned.1.call-start = ((), (), s32[]{:S(2)}) async-start(), calls=%async_computation.8 | async-start | bytes 4194304 | tf_op jit(solution)/shard_map/psum | solution.py:17
  424.8 45.7 %copy-start.6 = (f32[512,512]{1,0:T(8,128)}, f32[512,512]{1,0:T(8,128)S(1)}, u32[]{:S(2)}) copy-start(f32[512,512]{1,0:T(8,128)S(1)} %get-tuple-element.230) | copy-start | bytes 3145732
  478.0 135.1 %all-gather.9.cloned.1.call-start = ((), (), s32[]{:S(2)}) async-start(), calls=%async_computation.5 | async-start | bytes 2359296 | tf_op jit(solution)/shard_map/all_gather | solution.py:127
  579.6 3.4 copy-start.2
  586.3 75.4 %all-gather.11.cloned.1.call-start = ((), (), s32[]{:S(2)}) async-start(), calls=%async_computation.6 | async-start | bytes 2228224 | tf_op jit(solution)/shard_map/all_gather | solution.py:131
  614.7 285.9 %all-reduce.6.cloned.1.call-start = ((), (), s32[]{:S(2)}) async-start(), calls=%async_computation.7 | async-start | bytes 4194304 | tf_op jit(solution)/shard_map/psum | solution.py:17
  757.6 45.7 %copy-start.5 = (f32[512,512]{1,0:T(8,128)}, f32[512,512]{1,0:T(8,128)S(1)}, u32[]{:S(2)}) copy-start(f32[512,512]{1,0:T(8,128)S(1)} %get-tuple-element.229) | copy-start | bytes 3145732
  915.6 12.5 %copy-start.1 = (bf16[64,128,128]{2,1,0:T(8,128)(2,1)S(1)}, bf16[64,128,128]{2,1,0:T(8,128)(2,1)}, u32[]{:S(2)}) copy-start(bf16[64,128,128]{2,1,0:T(8,128)(2,1)} %param.17) | copy-start | bytes 6291460
Sparse Core Ops, SparseCore 0:
  250.4 30.9 all-gather.4
  283.6 46.2 all-gather.6
  478.1 89.7 all-reduce.7
  586.4 26.6 all-gather.8
  615.3 46.2 all-gather.10
  810.9 89.7 all-reduce.5
where the time goes:
time: 944 us; the launch traced here: 935 us
  waiting for transfers between devices  412 us (44%)
  other arithmetic  294 us (31%)
  local copies, waits for them, and re-layouts  111 us (12%)
  matrix products  70 us (7%)
  starting transfers between devices  28.8 us (3%)
  between operations  19.4 us (2%)
    psum x2, waiting for transfers between devices, broadcast(): return lax.psum(block, axis)  164 us
    another operation x29, other arithmetic, shards(): factor = jnp.linalg.cholesky(symmetric)  159 us
    all_to_all x1, waiting for transfers between devices, shards(): lax.all_to_all(send_tiles.reshape(owners, CAP, width, width), ('frow', 'f...  99.1 us
    all_gather x2, waiting for transfers between devices, shards(): lax.all_gather(panel[row_slot * width:(row_slot + 1) * width].astype(jnp....  86.9 us
    another operation x7, other arithmetic, shards(): lax.linalg.triangular_solve(factor, panel, left_side=False, lower=True, t...  82.1 us
    all_gather x2, waiting for transfers between devices, shards(): lax.all_gather(own_column.astype(jnp.bfloat16), 'fcol', axis=1, tiled=True)  57.8 us
    unnamed x15, local copies, waits for them, and re-layouts  37.9 us
    another operation x14, matrix products, shards(): lax.linalg.triangular_solve(factor, panel, left_side=False, lower=True, t...  23.7 us
  transfers between devices with their start and end apart: 9, of which 8 were waited for; matrix products, arithmetic and copies ran while one was open for 4% of the time, Pallas kernels for 0%

commit v1 on v0

--- a/solution.py
+++ b/solution.py
@@ -14,7 +14,7 @@
 
 def broadcast(block, axis, source):
     block = jnp.where(lax.axis_index(axis) == source, block, jnp.zeros_like(block))
-    return lax.psum(block, axis)
+    return jnp.sum(lax.all_gather(block, axis), axis=0)
 
 
 def place_tiles(received):

time: 944 us -> 1220 us (1.29)
  waiting for transfers between devices: 412 us -> 662 us
  other arithmetic: 294 us -> 331 us
    all_gather x0 -> x4, waiting for transfers between devices: none -> 413 us  [broadcast(): return jnp.sum(lax.all_gather(block, axis), axis=0)]
    psum x2 -> x0, waiting for transfers between devices: 164 us -> none  [broadcast(): return lax.psum(block, axis)]
    reduce_sum x0 -> x4, other arithmetic: none -> 37.6 us  [broadcast(): return jnp.sum(lax.all_gather(block, axis), axis=0)]
  transfers between devices with their start and end apart: 9 -> 11, of which waited for: 8 -> 10; matrix products, arithmetic and copies ran while one was open for 4% -> 5% of each run, Pallas kernels for 0% -> 0%
where the time goes in v1:
time: 1220 us; the launch traced here: 1210 us
  waiting for transfers between devices  662 us (54%)
  other arithmetic  331 us (27%)
  local copies, waits for them, and re-layouts  99.3 us (8%)
  matrix products  69.9 us (6%)
  starting transfers between devices  29 us (2%)
  between operations  19.3 us (2%)
    all_gather x4, waiting for transfers between devices, broadcast(): return jnp.sum(lax.all_gather(block, axis), axis=0)  413 us
    another operation x29, other arithmetic, shards(): factor = jnp.linalg.cholesky(symmetric)  158 us
    all_to_all x1, waiting for transfers between devices, shards(): lax.all_to_all(send_tiles.reshape(owners, CAP, width, width), ('frow', 'f...  99.1 us
    all_gather x2, waiting for transfers between devices, shards(): lax.all_gather(panel[row_slot * width:(row_slot + 1) * width].astype(jnp....  86.7 us
    another operation x7, other arithmetic, shards(): lax.linalg.triangular_solve(factor, panel, left_side=False, lower=True, t...  82.1 us
    all_gather x2, waiting for transfers between devices, shards(): lax.all_gather(own_column.astype(jnp.bfloat16), 'fcol', axis=1, tiled=True)  58 us
    reduce_sum x4, other arithmetic, broadcast(): return jnp.sum(lax.all_gather(block, axis), axis=0)  37.6 us
    unnamed x15, local copies, waits for them, and re-layouts  26.6 us
  transfers between devices with their start and end apart: 11, of which 10 were waited for; matrix products, arithmetic and copies ran while one was open for 5% of the time, Pallas kernels for 0%

profile of v1, /device:TPU:0, one launch (start us, length us, event | category | flops | bytes accessed | tf_op | source)
XLA Modules:
  0.0 1210.7 jit_solution(3138074219784912880)
XLA Ops:
  11.2 11.1 all-to-all-start
  62.8 99.1 %all-to-all-done.2 = bf16[128,2,128,128]{3,2,1,0:T(8,128)(2,1)} async-done(((bf16[128,2,128,128]{3,2,1,0:T(8,128)(2,1)}), bf16[128,2,128,128]{3,2,1,0:T(8,128)(2,1)}, u32[]{:S(2)}, u32[]{:S(2)}) %all-to-all-start.2) | async-done | bytes 8388640 | tf_op jit(solution)/shard_map/all_to_all | solution.py:75
  161.9 13.3 %fusion.6 = bf16[128,2,128,128]{3,2,1,0:T(8,128)(2,1)} fusion(s32[128,2,128]{2,1,0:T(2,128)S(1)} %get-tuple-element.80, bf16[128,2,128,128]{3,2,1,0:T(8,128)(2,1)} %all-to-all-done.2, s32[128,2,128]{2,1,0:T(2,128)S(1)} %get-tuple-element.79), kind=kOutput, calls=%fused_computation.21 | convolution fusion | flops 2164260864 | bytes 17039360 | tf_op jit(solution)/shard_map/abxj,abyj->abxy/dot_general | solution.py:29
  175.3 23.1 %copy.123 = bf16[32,8,128,128]{3,1,2,0:T(8,128)(2,1)} copy(bf16[32,8,128,128]{3,2,1,0:T(8,128)(2,1)} %bitcast.178) | data formatting | bytes 16777216
  198.4 11.9 copy.78
  219.7 17.6 %bitcast_add_fusion = f32[1024,2048]{1,0:T(8,128)} fusion(f32[128,8,16,128]{3,2,1,0:T(8,128)} %bitcast.175, f32[1,1024,1,2048]{3,2,1,0:T(1,128)} %param.16), kind=kLoop, calls=%fused_computation.14 | loop fusion | flops 2097152 | bytes 25165824 | tf_op jit(solution)/shard_map/add | solution.py:111
  239.1 31.1 %all-gather.9.cloned.1.call-done = bf16[1024,1024]{1,0:T(8,128)(2,1)} async-done(((bf16[1024,128]{1,0:T(8,128)(2,1)}), bf16[1024,1024]{1,0:T(8,128)(2,1)}) %all-gather.9.cloned.1.call-update) | async-done | bytes 2097168 | tf_op jit(solution)/shard_map/all_gather | solution.py:127
  275.2 43.5 %all-gather.11.cloned.1.call-done = bf16[2048,512]{1,0:T(8,128)(2,1)} async-done(((bf16[128,512]{1,0:T(8,128)(2,1)}), bf16[2048,512]{1,0:T(8,128)(2,1)}) %all-gather.11.cloned.1.call-update) | async-done | bytes 2097168 | tf_op jit(solution)/shard_map/all_gather | solution.py:131
  322.1 11.7 cholesky.286
  344.4 11.7 cholesky.305
  356.2 10.0 custom-call.28
  366.8 11.7 cholesky.326
  378.5 9.8 custom-call.29
  389.0 12.1 cholesky.343
  413.6 39.3 %custom-call.30 = f32[4,128,128]{1,2,0:T(8,128)S(1)} custom-call(f32[4,128,128]{2,1,0:T(8,128)S(1)} %get-tuple-element.47), custom_call_target="InvertDiagBlocksLowerTriangular" | custom-call | tf_op jit(solution)/shard_map/triangular_solve/custom-call.3 | solution.py:140
  474.5 103.1 %all-gather.15.cloned.1.call-done = bf16[16,8,128,512]{3,2,1,0:T(8,128)(2,1)} async-done(((bf16[1,8,128,512]{3,2,1,0:T(8,128)(2,1)}), bf16[16,8,128,512]{3,2,1,0:T(8,128)(2,1)}) %all-gather.15.cloned.1.call-update) | async-done | bytes 16777232 | tf_op jit(solution)/shard_map/all_gather | solution.py:17
  586.5 104.2 %all-gather.13.cloned.1.call-done = bf16[16,8,128,512]{3,2,1,0:T(8,128)(2,1)} async-done(((bf16[1,8,128,512]{3,2,1,0:T(8,128)(2,1)}), bf16[16,8,128,512]{3,2,1,0:T(8,128)(2,1)}) %all-gather.13.cloned.1.call-update) | async-done | bytes 16777232 | tf_op jit(solution)/shard_map/all_gather | solution.py:17
  690.7 9.9 reduce_sum.77
  702.0 9.9 convolution_subtract_fusion.1
  718.7 26.9 %all-gather.17.cloned.1.call-done = bf16[1024,1024]{1,0:T(8,128)(2,1)} async-done(((bf16[1024,128]{1,0:T(8,128)(2,1)}), bf16[1024,1024]{1,0:T(8,128)(2,1)}) %all-gather.17.cloned.1.call-update) | async-done | bytes 2097168 | tf_op jit(solution)/shard_map/all_gather | solution.py:127
  750.8 43.2 %all-gather.19.cloned.1.call-done = bf16[2048,512]{1,0:T(8,128)(2,1)} async-done(((bf16[128,512]{1,0:T(8,128)(2,1)}), bf16[2048,512]{1,0:T(8,128)(2,1)}) %all-gather.19.cloned.1.call-update) | async-done | bytes 2097168 | tf_op jit(solution)/shard_map/all_gather | solution.py:131
  797.4 11.7 cholesky.358
  819.7 11.9 cholesky.377
  831.6 9.8 custom-call.32
  842.1 11.7 cholesky.398
  853.9 9.8 custom-call.33
  864.3 12.1 cholesky.415
  889.5 39.3 %custom-call.34 = f32[4,128,128]{1,2,0:T(8,128)S(1)} custom-call(f32[4,128,128]{2,1,0:T(8,128)S(1)} %get-tuple-element.48), custom_call_target="InvertDiagBlocksLowerTriangular" | custom-call | tf_op jit(solution)/shard_map/triangular_solve/custom-call.3 | solution.py:140
  951.6 101.9 %all-gather.23.cloned.1.call-done = bf16[16,8,128,512]{3,2,1,0:T(8,128)(2,1)} async-done(((bf16[1,8,128,512]{3,2,1,0:T(8,128)(2,1)}), bf16[16,8,128,512]{3,2,1,0:T(8,128)(2,1)}) %all-gather.23.cloned.1.call-update) | async-done | bytes 16777232 | tf_op jit(solution)/shard_map/all_gather | solution.py:17
  1062.4 104.3 %all-gather.21.cloned.1.call-done = bf16[16,8,128,512]{3,2,1,0:T(8,128)(2,1)} async-done(((bf16[1,8,128,512]{3,2,1,0:T(8,128)(2,1)}), bf16[16,8,128,512]{3,2,1,0:T(8,128)(2,1)}) %all-gather.21.cloned.1.call-update) | async-done | bytes 16777232 | tf_op jit(solution)/shard_map/all_gather | solution.py:17
  1166.7 9.9 reduce_sum.79
  1191.1 12.5 %copy.99 = f32[1,1024,1,2048]{3,2,1,0:T(1,128)} copy(f32[1,1024,1,2048]{3,1,2,0:T(8,128)S(1)} %select_bitcast_fusion) | data formatting | bytes 16777216 | tf_op jit(solution)/shard_map/broadcast_in_dim | solution.py:167
  (188 shorter events, 217.7 us)
Async XLA Ops:
  6.5 18.5 %copy-start = (bf16[64,128,128]{2,1,0:T(8,128)(2,1)S(1)}, bf16[64,128,128]{2,1,0:T(8,128)(2,1)}, u32[]{:S(2)}) copy-start(bf16[64,128,128]{2,1,0:T(8,128)(2,1)} %param.17) | copy-start | bytes 6291460
  6.5 16.0 %copy-start.3 = (s32[64,128]{1,0:T(8,128)S(1)}, s32[64,128]{1,0:T(8,128)}, u32[]{:S(2)}) copy-start(s32[64,128]{1,0:T(8,128)} %param.19) | copy-start | bytes 98308
  6.5 16.7 %copy-start.4 = (s32[64,128]{1,0:T(8,128)S(1)}, s32[64,128]{1,0:T(8,128)}, u32[]{:S(2)}) copy-start(s32[64,128]{1,0:T(8,128)} %param.20) | copy-start | bytes 98308
  11.2 22.5 %all-to-all-start = ((s32[128,1,2]{2,1,0:T(1,128)}), s32[128,1,2]{2,1,0:T(1,128)S(1)}, u32[]{:S(2)}, u32[]{:S(2)}) async-start(s32[128,1,2]{2,1,0:T(1,128)} %bitcast.4), calls=%async_computation | async-start | bytes 131072 | tf_op jit(solution)/shard_map/all_to_all | solution.py:89
  33.7 20.5 %all-to-all-start.1 = ((s32[128,2,2,128]{3,1,2,0:T(2,128)}), s32[128,2,2,128]{3,1,2,0:T(2,128)S(1)}, u32[]{:S(2)}, u32[]{:S(2)}) async-start(s32[128,2,2,128]{3,1,2,0:T(2,128)} %pad_add_fusion), calls=%async_computation.1 | async-start | bytes 524288 | tf_op jit(solution)/shard_map/all_to_all | solution.py:82
  54.2 107.7 %all-to-all-start.2 = ((bf16[128,2,128,128]{3,2,1,0:T(8,128)(2,1)}), bf16[128,2,128,128]{3,2,1,0:T(8,128)(2,1)}, u32[]{:S(2)}, u32[]{:S(2)}) async-start(bf16[128,2,128,128]{3,2,1,0:T(8,128)(2,1)} %select_select_fusion), calls=%async_computation.2 | async-start | bytes 16777216 | tf_op jit(solution)/shard_map/all_to_all | solution.py:75
  61.3 208.9 %all-gather.9.cloned.1.call-start = ((), (), s32[]{:S(2)}) async-start(), calls=%async_computation.3 | async-start | bytes 2359296 | tf_op jit(solution)/shard_map/all_gather | solution.py:127
  239.1 79.6 %all-gather.11.cloned.1.call-start = ((), (), s32[]{:S(2)}) async-start(), calls=%async_computation.4 | async-start | bytes 2228224 | tf_op jit(solution)/shard_map/all_gather | solution.py:131
  271.8 305.8 %all-gather.15.cloned.1.call-start = ((), (), s32[]{:S(2)}) async-start(), calls=%async_computation.6 | async-start | bytes 17825792 | tf_op jit(solution)/shard_map/all_gather | solution.py:17
  413.6 45.7 %copy-start.6 = (f32[512,512]{1,0:T(8,128)}, f32[512,512]{1,0:T(8,128)S(1)}, u32[]{:S(2)}) copy-start(f32[512,512]{1,0:T(8,128)S(1)} %get-tuple-element.228) | copy-start | bytes 3145732
  466.7 223.9 %all-gather.13.cloned.1.call-start = ((), (), s32[]{:S(2)}) async-start(), calls=%async_computation.5 | async-start | bytes 17825792 | tf_op jit(solution)/shard_map/all_gather | solution.py:17
  467.3 278.3 %all-gather.17.cloned.1.call-start = ((), (), s32[]{:S(2)}) async-start(), calls=%async_computation.7 | async-start | bytes 2359296 | tf_op jit(solution)/shard_map/all_gather | solution.py:127
  711.9 3.4 copy-start.2
  718.7 75.3 %all-gather.19.cloned.1.call-start = ((), (), s32[]{:S(2)}) async-start(), calls=%async_computation.8 | async-start | bytes 2228224 | tf_op jit(solution)/shard_map/all_gather | solution.py:131
  747.2 306.3 %all-gather.23.cloned.1.call-start = ((), (), s32[]{:S(2)}) async-start(), calls=%async_computation.10 | async-start | bytes 17825792 | tf_op jit(solution)/shard_map/all_gather | solution.py:17
  889.5 45.7 %copy-start.5 = (f32[512,512]{1,0:T(8,128)}, f32[512,512]{1,0:T(8,128)S(1)}, u32[]{:S(2)}) copy-start(f32[512,512]{1,0:T(8,128)S(1)} %get-tuple-element.227) | copy-start | bytes 3145732
  942.6 224.1 %all-gather.21.cloned.1.call-start = ((), (), s32[]{:S(2)}) async-start(), calls=%async_computation.9 | async-start | bytes 17825792 | tf_op jit(solution)/shard_map/all_gather | solution.py:17
  1191.1 12.5 %copy-start.1 = (bf16[64,128,128]{2,1,0:T(8,128)(2,1)S(1)}, bf16[64,128,128]{2,1,0:T(8,128)(2,1)}, u32[]{:S(2)}) copy-start(bf16[64,128,128]{2,1,0:T(8,128)(2,1)} %param.17) | copy-start | bytes 6291460
Sparse Core Ops, SparseCore 0:
  239.2 30.9 all-gather.8
  272.3 46.2 all-gather.10
  466.8 110.6 all-gather.14
  579.6 111.0 all-gather.12
  718.8 26.7 all-gather.16
  747.6 46.2 all-gather.18
  942.8 110.6 all-gather.22
  1055.6 111.0 all-gather.20
